TPU v7x, 32 devices: a whole 2x2x4 slice. The times are simulated.
32 devices in a mesh: leaf: 4 (over y, x), src: 8 (over z, core).
Axes of the slice: x: 2, y: 2, z: 4, core: 2. Of those that a mesh axis runs over, the one named last changes fastest.
Arguments:
- src_cells: int32 [1024], P('src'), may hold values from 0 to 2047
- rec_cells: int32 [512], P('leaf'), may hold values from 0 to 511
- residual: float32 [1024, 512], P('src', 'leaf'), may hold values from -6 to 6
- pattern: int32 [12, 2], P('leaf'), may hold values 0 or 1
- leaf_lower: bfloat16 [2048, 512], P('leaf'), may hold values from -0.1875 to 0.1875
- leaf_upper: bfloat16 [2048, 512], P('leaf'), may hold values from -0.1875 to 0.1875
- leaf_inv: bfloat16 [16, 128, 128], P('leaf'), may hold values from -0.5 to 0.5
- anc_lower: bfloat16 [1024, 512], P('leaf'), may hold values from -0.125 to 0.125
- anc_upper: bfloat16 [2048, 256], P('leaf'), may hold values from -0.375 to 0.375
- sep_inv: bfloat16 [8, 128, 128], P('leaf'), may hold values from -0.5 to 0.5
- sep_lower: bfloat16 [8, 256, 128], P('leaf'), may hold values from -0.25 to 0.25
- sep_upper: bfloat16 [8, 128, 256], P('leaf'), may hold values from -0.375 to 0.375
Outputs:
- forward_field: float32 [1024, 2048], P('src', 'leaf')
- adjoint_field: float32 [1024, 2048], P('src', 'leaf')
- gradient: float32 [2048], P(('leaf', 'src'))
Inputs may be any that keep to these rules, and one draw needn't show every extreme that they name: src_cells holds 512 d + c for a source in interior cell c of subdomain d. rec_cells holds a receiver's cell within the subdomain of its block of 128 entries.
All inputs are finite; a program needn't handle non-finite values. No bound on the sum of `pattern` on one device may be relied on, other than what follows from the above.
Results may differ from a plain program's by a relative error of at most 0.0068.
Values may be sent and summed in bfloat16 or wider, within the bound.
No kernel may reach another device: no remote copies, remote signals or barrier semaphores. Data moves between devices by JAX's collectives and lax.ppermute only.
A program may use at most 64 MiB of HBM per device.

v0:
```python
import math
import jax
import jax.numpy as jnp
from jax import lax
from jax.sharding import PartitionSpec as P


def across(former, latter):
    return lax.dot_general(
        former, latter, (((1,), (1,)), ((), ())), preferred_element_type=jnp.float32
    )


def plain_dot(former, latter):
    return jnp.dot(former, latter, preferred_element_type=jnp.float32)


def as_half(values):
    return values.astype(jnp.bfloat16)


def lower_solve(right_side, lower, block_size, block_count):
    solved = []
    for index in range(block_count):
        segment = right_side[:, index * block_size : (index + 1) * block_size]
        if index:
            earlier = as_half(jnp.concatenate(solved, axis=1))
            segment = segment - across(
                earlier, lower[index * block_size : (index + 1) * block_size, : index * block_size]
            )
        solved.append(segment)
    return jnp.concatenate(solved, axis=1)


def upper_solve(right_side, upper, inverse, block_size, block_count):
    behind = []
    for index in reversed(range(block_count)):
        segment = right_side[:, index * block_size : (index + 1) * block_size]
        if behind:
            segment = segment - across(
                as_half(jnp.concatenate(behind, axis=1)),
                upper[index * block_size : (index + 1) * block_size, (index + 1) * block_size :],
            )
        behind.insert(0, across(as_half(segment), inverse[index]))
    return jnp.concatenate(behind, axis=1)


def upper_t_solve(right_side, upper, inverse, block_size, block_count):
    solved = []
    for index in range(block_count):
        segment = right_side[:, index * block_size : (index + 1) * block_size]
        if index:
            earlier = as_half(jnp.concatenate(solved, axis=1))
            segment = segment - plain_dot(
                earlier, upper[: index * block_size, index * block_size : (index + 1) * block_size]
            )
        solved.append(plain_dot(as_half(segment), inverse[index]))
    return jnp.concatenate(solved, axis=1)


def lower_t_solve(right_side, lower, block_size, block_count):
    behind = []
    for index in reversed(range(block_count)):
        segment = right_side[:, index * block_size : (index + 1) * block_size]
        if behind:
            segment = segment - plain_dot(
                as_half(jnp.concatenate(behind, axis=1)),
                lower[(index + 1) * block_size :, index * block_size : (index + 1) * block_size],
            )
        behind.insert(0, segment)
    return jnp.concatenate(behind, axis=1)


def climb(starts, handlers, levels, block_size, device):
    contributions = list(starts)
    results = [[] for member in starts]
    for height in range(1, levels + 1):
        lowest = (height - 1) * block_size
        piece = jnp.stack([summed[:, lowest : lowest + block_size] for summed in contributions])
        gathered = lax.all_gather(piece[None], "leaf", axis=0, tiled=True)
        first = device >> height << height
        total = jnp.sum(lax.dynamic_slice_in_dim(gathered, first, 1 << height, 0), axis=0)
        owner = device % (1 << height) == 0
        member = 0
        node_value, coupling = handlers[member](height, total[member])
        results[member].append(node_value)
        contributions[member] = contributions[member] + jnp.where(
            owner, coupling, jnp.zeros_like(coupling)
        )
    return results


def descend(node_values, handlers, levels, block_size, device, sources):
    known = [jnp.zeros((sources, levels * block_size), jnp.float32) for member in node_values]
    for height in range(levels, 0, -1):
        outgoing = jnp.stack([as_half(handlers[0](height, known[0], node_values[0][height - 1]))])
        gathered = lax.all_gather(outgoing[None], "leaf", axis=0, tiled=True)
        owner_index = device >> height << height
        piece = lax.dynamic_index_in_dim(gathered, owner_index, 0, keepdims=False).astype(
            jnp.float32
        )
        known = [lax.dynamic_update_slice_in_dim(known[0], piece[0], (height - 1) * block_size, 1)]
    return known


def shards(
    src_cells,
    rec_cells,
    residual,
    pattern,
    leaf_lower,
    leaf_upper,
    leaf_inv,
    anc_lower,
    anc_upper,
    sep_inv,
    sep_lower,
    sep_upper,
):
    levels = lax.axis_size("leaf").bit_length() - 1
    device = lax.axis_index("leaf")
    block_size = leaf_inv.shape[1]
    block_count = leaf_inv.shape[0]
    cell_count = leaf_lower.shape[1]
    source_count = src_cells.shape[0]
    factor = 1.0 / math.sqrt(source_count * lax.axis_size("src"))
    present = pattern.astype(jnp.float32)

    def level_mask(height):
        level_row = present[height] * (jnp.arange(1, levels + 1) > height).astype(jnp.float32)
        return jnp.repeat(level_row, block_size)

    columns = lax.broadcasted_iota(jnp.int32, (source_count, cell_count), 1)
    forcing = (src_cells[:, None] - device * cell_count == columns).astype(jnp.float32)
    receiver_hits = (
        rec_cells[:, None] == lax.broadcasted_iota(jnp.int32, (rec_cells.shape[0], cell_count), 1)
    ).astype(jnp.float32)
    adjoint_rhs = jnp.dot(residual, receiver_hits, precision=lax.Precision.HIGHEST)

    def forward_up(height, summed):
        node_value = -summed
        return (node_value, across(as_half(node_value), sep_lower[height - 1]) * level_mask(height))

    def adjoint_up(height, summed):
        node_value = plain_dot(as_half(-summed), sep_inv[height - 1])
        return (
            node_value,
            plain_dot(as_half(node_value), sep_upper[height - 1]) * level_mask(height),
        )

    def forward_down(height, above, node_value):
        right_side = node_value - across(as_half(above * level_mask(height)), sep_upper[height - 1])
        return across(as_half(right_side), sep_inv[height - 1])

    def adjoint_down(height, above, node_value):
        return node_value - plain_dot(as_half(above * level_mask(height)), sep_lower[height - 1])

    base_mask = level_mask(0)
    y_leaf = lower_solve(forcing, leaf_lower, block_size, block_count)
    forward_start = across(as_half(y_leaf), anc_lower) * base_mask
    z_leaf = upper_t_solve(adjoint_rhs, leaf_upper, leaf_inv, block_size, block_count)
    adjoint_start = plain_dot(as_half(z_leaf), anc_upper) * base_mask
    forward_values = climb([forward_start], [forward_up], levels, block_size, device)
    forward_above = descend(
        forward_values, [forward_down], levels, block_size, device, source_count
    )[0]
    adjoint_values = climb([adjoint_start], [adjoint_up], levels, block_size, device)
    adjoint_above = descend(
        adjoint_values, [adjoint_down], levels, block_size, device, source_count
    )[0]
    forward_remain = y_leaf - across(as_half(forward_above * base_mask), anc_upper)
    forward_field = upper_solve(forward_remain, leaf_upper, leaf_inv, block_size, block_count)
    adjoint_remain = z_leaf - plain_dot(as_half(adjoint_above * base_mask), anc_lower)
    adjoint_field = lower_t_solve(adjoint_remain, leaf_lower, block_size, block_count)
    partial_gradient = jnp.sum(forward_field * adjoint_field, axis=0)
    gradient = lax.psum_scatter(partial_gradient, "src", scatter_dimension=0, tiled=True) * factor
    return (forward_field, adjoint_field, gradient)


def solution(mesh):
    in_specs = (
        P("src"),
        P("leaf"),
        P("src", "leaf"),
        P("leaf", None),
        P("leaf", None),
        P("leaf", None),
        P("leaf", None, None),
        P("leaf", None),
        P("leaf", None),
        P("leaf", None, None),
        P("leaf", None, None),
        P("leaf", None, None),
    )
    out_specs = (P("src", "leaf"), P("src", "leaf"), P(("leaf", "src")))
    return jax.shard_map(shards, mesh=mesh, in_specs=in_specs, out_specs=out_specs, check_vma=False)
```

profile of v0, /device:TPU:0, one launch (start us, length us, event | category | flops | bytes accessed | tf_op | source)
XLA Modules:
  0.0 98.7 jit_solution(13294854775724279794)
XLA Ops:
  0.7 0.7 broadcast_subtract_fusion
  1.4 0.9 fusion.189
  2.7 0.7 copy-done.9
  4.0 10.6 %all-gather = f32[512,128]{1,0:T(8,128)S(1)} all-gather(f32[128,128]{1,0:T(8,128)S(1)} %slice.198), channel_id=2, replica_groups=mesh['leaf'=4,'src'=8] {'leaf'}, dimensions={0}, use_global_device_ids=true | all-gather | bytes 327680 | tf_op jit(solution)/shard_map/all_gather | solution.py:80
  14.6 0.4 convolution_bitcast_fusion
  15.0 0.5 copy-done.3
  15.7 0.3 fusion.181
  16.0 0.4 fusion.184
  16.4 0.4 fusion.13
  17.0 9.0 %all-gather.4 = f32[512,128]{1,0:T(8,128)S(1)} all-gather(f32[128,128]{1,0:T(8,128)S(1)} %slice.210), channel_id=6, replica_groups=mesh['leaf'=4,'src'=8] {'leaf'}, dimensions={0}, use_global_device_ids=true | all-gather | bytes 327680 | tf_op jit(solution)/shard_map/all_gather | solution.py:80
  26.0 0.8 copy-done.4
  27.1 0.8 copy-done.1
  28.2 8.1 %all-gather.1 = f32[512,128]{1,0:T(8,128)S(1)} all-gather(f32[128,128]{1,0:T(8,128)S(1)} %get-tuple-element.16), channel_id=3, replica_groups=mesh['leaf'=4,'src'=8] {'leaf'}, dimensions={0}, use_global_device_ids=true | all-gather | bytes 327680 | tf_op jit(solution)/shard_map/all_gather | solution.py:80
  36.6 8.7 %all-gather.2 = bf16[512,128]{1,0:T(8,128)(2,1)S(1)} all-gather(bf16[128,128]{1,0:T(8,128)(2,1)S(1)} %convolution_convert_fusion.1), channel_id=4, replica_groups=mesh['leaf'=4,'src'=8] {'leaf'}, dimensions={0}, use_global_device_ids=true | all-gather | bytes 163840 | tf_op jit(solution)/shard_map/all_gather | solution.py:97
  45.7 7.3 %all-gather.3 = bf16[512,128]{1,0:T(8,128)(2,1)S(1)} all-gather(bf16[128,128]{1,0:T(8,128)(2,1)S(1)} %convolution_convert_fusion), channel_id=5, replica_groups=mesh['leaf'=4,'src'=8] {'leaf'}, dimensions={0}, use_global_device_ids=true | all-gather | bytes 163840 | tf_op jit(solution)/shard_map/all_gather | solution.py:97
  54.2 9.2 %all-gather.5 = f32[512,128]{1,0:T(8,128)S(1)} all-gather(f32[128,128]{1,0:T(8,128)S(1)} %get-tuple-element.15), channel_id=7, replica_groups=mesh['leaf'=4,'src'=8] {'leaf'}, dimensions={0}, use_global_device_ids=true | all-gather | bytes 327680 | tf_op jit(solution)/shard_map/all_gather | solution.py:80
  63.7 7.3 %all-gather.6 = bf16[512,128]{1,0:T(8,128)(2,1)S(1)} all-gather(bf16[128,128]{1,0:T(8,128)(2,1)S(1)} %fusion.5), channel_id=8, replica_groups=mesh['leaf'=4,'src'=8] {'leaf'}, dimensions={0}, use_global_device_ids=true | all-gather | bytes 163840 | tf_op jit(solution)/shard_map/all_gather | solution.py:97
  71.2 8.6 %all-gather.7 = bf16[512,128]{1,0:T(8,128)(2,1)S(1)} all-gather(bf16[128,128]{1,0:T(8,128)(2,1)S(1)} %fusion.6), channel_id=9, replica_groups=mesh['leaf'=4,'src'=8] {'leaf'}, dimensions={0}, use_global_device_ids=true | all-gather | bytes 163840 | tf_op jit(solution)/shard_map/all_gather | solution.py:97
  81.0 0.8 copy.21
  81.8 0.8 copy.22
  82.7 13.6 %all-reduce.2 = f32[512]{0:T(512)S(1)} all-reduce(f32[512]{0:T(512)S(1)} %get-tuple-element.12), channel_id=10, replica_groups=mesh['leaf'=4,'src'=8] {'src'}, use_global_device_ids=true, to_apply=%region_5.6.clone | all-reduce | flops 512 | bytes 4096
  96.3 0.7 copy-done.11
  96.9 0.6 dynamic-slice
  98.1 0.6 dynamic-slice_multiply_fusion
  (66 shorter events, 5.4 us)
Async XLA Ops:
  0.6 16.1 %copy-start = (bf16[512,256]{1,0:T(8,128)(2,1)S(1)}, bf16[512,256]{1,0:T(8,128)(2,1)}, u32[]{:S(2)}) copy-start(bf16[512,256]{1,0:T(8,128)(2,1)} %param.20) | copy-start | bytes 786436
  0.6 1.7 %copy-start.7 = (bf16[512,512]{1,0:T(8,128)(2,1)S(1)}, bf16[512,512]{1,0:T(8,128)(2,1)}, u32[]{:S(2)}) copy-start(bf16[512,512]{1,0:T(8,128)(2,1)} %param.16) | copy-start | bytes 1572868
  2.5 1.2 %copy-start.5 = (bf16[256,512]{1,0:T(8,128)(2,1)S(1)}, bf16[256,512]{1,0:T(8,128)(2,1)}, u32[]{:S(2)}) copy-start(bf16[256,512]{1,0:T(8,128)(2,1)} %param.19) | copy-start | bytes 786436
  2.7 0.7 copy-start.9
  3.7 10.9 %copy-start.8 = (f32[128,128]{1,0:T(8,128)S(1)}, f32[128,128]{1,0:T(8,128)}, u32[]{:S(2)}) copy-start(f32[128,128]{1,0:T(8,128)} %param.14) | copy-start | bytes 196612
  3.7 10.9 %copy-start.10 = (s32[128]{0:T(128)S(1)}, s32[128]{0:T(128)}, u32[]{:S(2)}) copy-start(s32[128]{0:T(128)} %param.13) | copy-start | bytes 1540
  3.9 11.7 %copy-start.6 = (bf16[512,512]{1,0:T(8,128)(2,1)S(1)}, bf16[512,512]{1,0:T(8,128)(2,1)}, u32[]{:S(2)}) copy-start(bf16[512,512]{1,0:T(8,128)(2,1)} %param.17) | copy-start | bytes 1572868
  14.6 0.9 copy-start.3
  26.0 0.8 copy-start.4
  26.0 0.9 copy-start.2
  27.0 0.9 copy-start.1
  96.2 0.7 copy-start.11
where the time goes:
time: 99.2 us; the launch traced here: 98.7 us
  blocking collectives  82.3 us (83%)
  matrix products  6.91 us (7%)
  local copies, waits for them, and re-layouts  6.16 us (6%)
  between operations  1.7 us (2%)
  other arithmetic  1.61 us (2%)
    all_gather x4, blocking collectives, climb(): gathered = lax.all_gather(piece[None], 'leaf', axis=0, tiled=True)  36.8 us
    all_gather x4, blocking collectives, descend(): gathered = lax.all_gather(outgoing[None], 'leaf', axis=0, tiled=True)  31.9 us
    unnamed x1, blocking collectives  13.6 us
    unnamed x27, local copies, waits for them, and re-layouts  5.69 us
    dot_general x12, matrix products, across(): lax.dot_general(former, latter, (((1,), (1,)), ((), ())), preferred_eleme...  3.42 us
    dot_general x14, matrix products, plain_dot(): return jnp.dot(former, latter, preferred_element_type=jnp.float32)  3.11 us

commit v1 on v0

--- a/solution.py
+++ b/solution.py
@@ -77,7 +77,30 @@
     for height in range(1, levels + 1):
         lowest = (height - 1) * block_size
         piece = jnp.stack([summed[:, lowest : lowest + block_size] for summed in contributions])
-        gathered = lax.all_gather(piece[None], "leaf", axis=0, tiled=True)
+        size, index_2, extent = (
+            lax.axis_size("leaf"),
+            lax.axis_index("leaf"),
+            piece[None].shape[0],
+        )
+        ahead = [(i, (i + 1) % size) for i in range(size)]
+        downward = [(i, (i - 1) % size) for i in range(size)]
+        filled = jnp.zeros(
+            (*piece[None].shape[:0], size * extent, *piece[None].shape[0 + 1 :]), piece[None].dtype
+        )
+        filled = lax.dynamic_update_slice_in_dim(filled, piece[None], index_2 * extent, axis=0)
+        from_left = from_right = piece[None]
+        middle = size // 2
+        for step in range(1, middle + 1):
+            from_left = lax.ppermute(from_left, "leaf", ahead)
+            filled = lax.dynamic_update_slice_in_dim(
+                filled, from_left, (index_2 - step) % size * extent, axis=0
+            )
+            if step < size - middle:
+                from_right = lax.ppermute(from_right, "leaf", downward)
+                filled = lax.dynamic_update_slice_in_dim(
+                    filled, from_right, (index_2 + step) % size * extent, axis=0
+                )
+        gathered = filled
         first = device >> height << height
         total = jnp.sum(lax.dynamic_slice_in_dim(gathered, first, 1 << height, 0), axis=0)
         owner = device % (1 << height) == 0

time: 99.2 us -> 89.4 us (0.901)
  blocking collectives: 82.3 us -> 45.7 us
  starting transfers between devices: 0 us -> 17.8 us
  waiting for transfers between devices: 0 us -> 7.1 us
  local copies, waits for them, and re-layouts: 6.16 us -> 7.94 us
    all_gather x4 -> x0, blocking collectives: 36.8 us -> none  [climb(): gathered = lax.all_gather(piece[None], 'leaf', axis=0, tiled=True)]
    ppermute x0 -> x12, starting transfers between devices: none -> 17.8 us  [the longest x8 9.63 us: climb(): from_left = lax.ppermute(from_left, 'leaf', ahead)]
    ppermute x0 -> x12, waiting for transfers between devices: none -> 7.1 us  [the longest x8 6.5 us: climb(): from_left = lax.ppermute(from_left, 'leaf', ahead)]
    unnamed x27 -> x25, local copies, waits for them, and re-layouts: 5.69 us -> 6.41 us
  transfers between devices with their start and end apart: 0 -> 12, of which waited for: 0 -> 5; matrix products, arithmetic and copies ran while one was open for 0% -> 6% of each run, Pallas kernels for 0% -> 0%
where the time goes in v1:
time: 89.4 us; the launch traced here: 89 us
  blocking collectives  45.7 us (51%)
  starting transfers between devices  17.8 us (20%)
  local copies, waits for them, and re-layouts  7.94 us (9%)
  waiting for transfers between devices  7.1 us (8%)
  matrix products  6.92 us (8%)
  between operations  1.87 us (2%)
  other arithmetic  1.65 us (2%)
    all_gather x4, blocking collectives, descend(): gathered = lax.all_gather(outgoing[None], 'leaf', axis=0, tiled=True)  32.1 us
    unnamed x1, blocking collectives  13.6 us
    ppermute x8, starting transfers between devices, climb(): from_left = lax.ppermute(from_left, 'leaf', ahead)  9.63 us
    ppermute x4, starting transfers between devices, climb(): from_right = lax.ppermute(from_right, 'leaf', downward)  8.18 us
    ppermute x8, waiting for transfers between devices, climb(): from_left = lax.ppermute(from_left, 'leaf', ahead)  6.5 us
    unnamed x25, local copies, waits for them, and re-layouts  6.41 us
    dot_general x12, matrix products, across(): lax.dot_general(former, latter, (((1,), (1,)), ((), ())), preferred_eleme...  3.43 us
    dot_general x14, matrix products, plain_dot(): return jnp.dot(former, latter, preferred_element_type=jnp.float32)  3.12 us
  transfers between devices with their start and end apart: 12, of which 5 were waited for; matrix products, arithmetic and copies ran while one was open for 6% of the time, Pallas kernels for 0%

profile of v1, /device:TPU:0, one launch (start us, length us, event | category | flops | bytes accessed | tf_op | source)
XLA Modules:
  0.0 89.0 jit_solution(12822596794534241850)
XLA Ops:
  1.5 0.9 %fusion.196 = (bf16[128,128]{0,1:T(8,128)(2,1)S(1)}, f32[128,128]{0,1:T(8,128)S(1)}) fusion(bf16[512,512]{1,0:T(8,128)(2,1)} %param.16, f32[128,512]{0,1:T(8,128)S(1)} %fusion.15), kind=kOutput, calls=%fused_computation.229 | convolution fusion | flops 4227072 | bytes 229376 | tf_op jit(solution)/shard_map/dot_general | solution.py:9
  3.8 3.0 %collective-permute-start = (f32[1,1,128,128]{3,2,1,0:T(8,128)S(1)}, f32[1,1,128,128]{3,2,1,0:T(8,128)S(1)}, u32[]{:S(2)}, u32[]{:S(2)}) collective-permute-start(f32[1,1,128,128]{3,2,1,0:T(8,128)S(1)} %slice_bitcast_fusion.1), channel_id=1, source_target_pairs={{0,8},{8,16},{16,24},{24,0},{1,9},{9,17},{17,25},{25,1},{2,10},{10... | collective-permute-start | bytes 196616 | tf_op jit(solution)/shard_map/ppermute | solution.py:94
  6.8 1.0 %collective-permute-start.1 = (f32[1,1,128,128]{3,2,1,0:T(8,128)S(1)}, f32[1,1,128,128]{3,2,1,0:T(8,128)S(1)}, u32[]{:S(2)}, u32[]{:S(2)}) collective-permute-start(f32[1,1,128,128]{3,2,1,0:T(8,128)S(1)} %slice_bitcast_fusion.1), channel_id=1, source_target_pairs={{0,24},{8,0},{16,8},{24,16},{1,25},{9,1},{17,9},{25,17},{2,26},{10... | collective-permute-start | bytes 196616 | tf_op jit(solution)/shard_map/ppermute | solution.py:99
  10.4 1.1 %collective-permute-start.6 = (f32[1,1,128,128]{3,2,1,0:T(8,128)S(1)}, f32[1,1,128,128]{3,2,1,0:T(8,128)}, u32[]{:S(2)}, u32[]{:S(2)}) collective-permute-start(f32[1,1,128,128]{3,2,1,0:T(8,128)S(1)} %slice_bitcast_fusion), channel_id=1, source_target_pairs={{0,8},{8,16},{16,24},{24,0},{1,9},{9,17},{17,25},{25,1},{2,10},{10... | collective-permute-start | bytes 196616 | tf_op jit(solution)/shard_map/ppermute | solution.py:94
  11.4 1.9 %collective-permute-start.7 = (f32[1,1,128,128]{3,2,1,0:T(8,128)S(1)}, f32[1,1,128,128]{3,2,1,0:T(8,128)S(1)}, u32[]{:S(2)}, u32[]{:S(2)}) collective-permute-start(f32[1,1,128,128]{3,2,1,0:T(8,128)S(1)} %slice_bitcast_fusion), channel_id=1, source_target_pairs={{0,24},{8,0},{16,8},{24,16},{1,25},{9,1},{17,9},{25,17},{2,26},{10... | collective-permute-start | bytes 196616 | tf_op jit(solution)/shard_map/ppermute | solution.py:99
  13.5 0.8 copy-done.2
  14.6 1.2 %dynamic-slice = u32[1]{0:T(128)} dynamic-slice(u32[32]{0:T(128)} %constant.97, u32[]{:T(128)S(6)} %add.108), dynamic_slice_sizes={1} | dynamic-slice | bytes 12
  17.0 2.9 %collective-permute-start.8 = (f32[1,1,128,128]{3,2,1,0:T(8,128)}, f32[1,1,128,128]{3,2,1,0:T(8,128)S(1)}, u32[]{:S(2)}, u32[]{:S(2)}) collective-permute-start(f32[1,1,128,128]{3,2,1,0:T(8,128)} %collective-permute-done.6), channel_id=1, source_target_pairs={{0,8},{8,16},{16,24},{24,0},{1,9},{9,17},{17,25},{25,1},{2,10},{10... | collective-permute-start | bytes 196616 | tf_op jit(solution)/shard_map/ppermute | solution.py:94
  19.9 0.9 constant_dynamic-update-slice_fusion.6
  20.9 0.8 collective-permute-done.2
  22.1 2.8 %collective-permute-start.4 = (f32[1,1,128,128]{3,2,1,0:T(8,128)S(1)}, f32[1,1,128,128]{3,2,1,0:T(8,128)S(1)}, u32[]{:S(2)}, u32[]{:S(2)}) collective-permute-start(f32[1,1,128,128]{3,2,1,0:T(8,128)S(1)} %get-tuple-element.15), channel_id=1, source_target_pairs={{0,24},{8,0},{16,8},{24,16},{1,25},{9,1},{17,9},{25,17},{2,26},{10... | collective-permute-start | bytes 196616 | tf_op jit(solution)/shard_map/ppermute | solution.py:99
  25.0 0.8 copy-done.5
  27.4 2.4 %collective-permute-start.10 = (f32[1,1,128,128]{3,2,1,0:T(8,128)S(1)}, f32[1,1,128,128]{3,2,1,0:T(8,128)S(1)}, u32[]{:S(2)}, u32[]{:S(2)}) collective-permute-start(f32[1,1,128,128]{3,2,1,0:T(8,128)S(1)} %get-tuple-element.13), channel_id=1, source_target_pairs={{0,24},{8,0},{16,8},{24,16},{1,25},{9,1},{17,9},{25,17},{2,26},{10... | collective-permute-start | bytes 196616 | tf_op jit(solution)/shard_map/ppermute | solution.py:99
  30.4 2.0 %collective-permute-done.9 = f32[1,1,128,128]{3,2,1,0:T(8,128)S(1)} collective-permute-done((f32[1,1,128,128]{3,2,1,0:T(8,128)S(1)}, f32[1,1,128,128]{3,2,1,0:T(8,128)S(1)}, u32[]{:S(2)}, u32[]{:S(2)}) %collective-permute-start.9) | collective-permute-done | bytes 65568 | tf_op jit(solution)/shard_map/ppermute | solution.py:94
  32.4 0.9 %collective-permute-start.11 = (f32[1,1,128,128]{3,2,1,0:T(8,128)S(1)}, f32[1,1,128,128]{3,2,1,0:T(8,128)S(1)}, u32[]{:S(2)}, u32[]{:S(2)}) collective-permute-start(f32[1,1,128,128]{3,2,1,0:T(8,128)S(1)} %collective-permute-done.9), channel_id=1, source_target_pairs={{0,8},{8,16},{16,24},{24,0},{1,9},{9,17},{17,25},{25,1},{2,10},{10... | collective-permute-start | bytes 196616 | tf_op jit(solution)/shard_map/ppermute | solution.py:94
  34.0 1.0 %collective-permute-done.5 = f32[1,1,128,128]{3,2,1,0:T(8,128)S(1)} collective-permute-done((f32[1,1,128,128]{3,2,1,0:T(8,128)S(1)}, f32[1,1,128,128]{3,2,1,0:T(8,128)S(1)}, u32[]{:S(2)}, u32[]{:S(2)}) %collective-permute-start.5) | collective-permute-done | bytes 65568 | tf_op jit(solution)/shard_map/ppermute | solution.py:94
  35.0 2.6 %collective-permute-done.11 = f32[1,1,128,128]{3,2,1,0:T(8,128)S(1)} collective-permute-done((f32[1,1,128,128]{3,2,1,0:T(8,128)S(1)}, f32[1,1,128,128]{3,2,1,0:T(8,128)S(1)}, u32[]{:S(2)}, u32[]{:S(2)}) %collective-permute-start.11) | collective-permute-done | bytes 65568 | tf_op jit(solution)/shard_map/ppermute | solution.py:94
  37.8 8.9 %all-gather.2 = bf16[512,128]{1,0:T(8,128)(2,1)S(1)} all-gather(bf16[128,128]{1,0:T(8,128)(2,1)S(1)} %fusion.4), channel_id=4, replica_groups=mesh['leaf'=4,'src'=8] {'leaf'}, dimensions={0}, use_global_device_ids=true | all-gather | bytes 163840 | tf_op jit(solution)/shard_map/all_gather | solution.py:120
  46.8 7.3 %all-gather.3 = bf16[512,128]{1,0:T(8,128)(2,1)S(1)} all-gather(bf16[128,128]{1,0:T(8,128)(2,1)S(1)} %fusion.5), channel_id=5, replica_groups=mesh['leaf'=4,'src'=8] {'leaf'}, dimensions={0}, use_global_device_ids=true | all-gather | bytes 163840 | tf_op jit(solution)/shard_map/all_gather | solution.py:120
  55.0 8.7 %all-gather = bf16[512,128]{1,0:T(8,128)(2,1)S(1)} all-gather(bf16[128,128]{1,0:T(8,128)(2,1)S(1)} %convolution_convert_fusion.1), channel_id=2, replica_groups=mesh['leaf'=4,'src'=8] {'leaf'}, dimensions={0}, use_global_device_ids=true | all-gather | bytes 163840 | tf_op jit(solution)/shard_map/all_gather | solution.py:120
  64.0 7.3 %all-gather.1 = bf16[512,128]{1,0:T(8,128)(2,1)S(1)} all-gather(bf16[128,128]{1,0:T(8,128)(2,1)S(1)} %convolution_convert_fusion), channel_id=3, replica_groups=mesh['leaf'=4,'src'=8] {'leaf'}, dimensions={0}, use_global_device_ids=true | all-gather | bytes 163840 | tf_op jit(solution)/shard_map/all_gather | solution.py:120
  73.1 0.8 copy.21
  74.0 0.8 copy.22
  74.8 13.6 %all-reduce.2 = f32[512]{0:T(512)S(1)} all-reduce(f32[512]{0:T(512)S(1)} %get-tuple-element.16), channel_id=6, replica_groups=mesh['leaf'=4,'src'=8] {'src'}, use_global_device_ids=true, to_apply=%region_5.6.clone | all-reduce | flops 512 | bytes 4096
  (103 shorter events, 12.6 us)
Async XLA Ops:
  0.6 2.9 %copy-start = (bf16[256,512]{1,0:T(8,128)(2,1)S(1)}, bf16[256,512]{1,0:T(8,128)(2,1)}, u32[]{:S(2)}) copy-start(bf16[256,512]{1,0:T(8,128)(2,1)} %param.19) | copy-start | bytes 786436
  0.6 1.7 %copy-start.7 = (bf16[512,512]{1,0:T(8,128)(2,1)S(1)}, bf16[512,512]{1,0:T(8,128)(2,1)}, u32[]{:S(2)}) copy-start(bf16[512,512]{1,0:T(8,128)(2,1)} %param.16) | copy-start | bytes 1572868
  2.5 0.7 copy-start.9
  3.5 4.9 %copy-start.6 = (bf16[512,512]{1,0:T(8,128)(2,1)S(1)}, bf16[512,512]{1,0:T(8,128)(2,1)}, u32[]{:S(2)}) copy-start(bf16[512,512]{1,0:T(8,128)(2,1)} %param.17) | copy-start | bytes 1572868
  3.7 4.1 %copy-start.8 = (f32[128,128]{1,0:T(8,128)S(1)}, f32[128,128]{1,0:T(8,128)}, u32[]{:S(2)}) copy-start(f32[128,128]{1,0:T(8,128)} %param.14) | copy-start | bytes 196612
  3.8 4.1 %copy-start.10 = (s32[128]{0:T(128)S(1)}, s32[128]{0:T(128)}, u32[]{:S(2)}) copy-start(s32[128]{0:T(128)} %param.13) | copy-start | bytes 1540
  3.8 4.4 %copy-start.4 = (bf16[4,128,128]{2,1,0:T(8,128)(2,1)S(1)}, bf16[4,128,128]{2,1,0:T(8,128)(2,1)}, u32[]{:S(2)}) copy-start(bf16[4,128,128]{2,1,0:T(8,128)(2,1)} %param.18) | copy-start | bytes 393220
  3.8 12.7 %collective-permute-start = (f32[1,1,128,128]{3,2,1,0:T(8,128)S(1)}, f32[1,1,128,128]{3,2,1,0:T(8,128)S(1)}, u32[]{:S(2)}, u32[]{:S(2)}) collective-permute-start(f32[1,1,128,128]{3,2,1,0:T(8,128)S(1)} %slice_bitcast_fusion.1), channel_id=1, source_target_pairs={{0,8},{8,16},{16,24},{24,0},{1,9},{9,17},{17,25},{25,1},{2,10},{10... | collective-permute-start | bytes 196616 | tf_op jit(solution)/shard_map/ppermute | solution.py:94
  6.8 14.0 %collective-permute-start.1 = (f32[1,1,128,128]{3,2,1,0:T(8,128)S(1)}, f32[1,1,128,128]{3,2,1,0:T(8,128)S(1)}, u32[]{:S(2)}, u32[]{:S(2)}) collective-permute-start(f32[1,1,128,128]{3,2,1,0:T(8,128)S(1)} %slice_bitcast_fusion.1), channel_id=1, source_target_pairs={{0,24},{8,0},{16,8},{24,16},{1,25},{9,1},{17,9},{25,17},{2,26},{10... | collective-permute-start | bytes 196616 | tf_op jit(solution)/shard_map/ppermute | solution.py:99
  9.2 1.0 %copy-start.1 = (bf16[512,256]{1,0:T(8,128)(2,1)S(1)}, bf16[512,256]{1,0:T(8,128)(2,1)}, u32[]{:S(2)}) copy-start(bf16[512,256]{1,0:T(8,128)(2,1)} %param.20) | copy-start | bytes 786436
  10.4 6.7 %collective-permute-start.6 = (f32[1,1,128,128]{3,2,1,0:T(8,128)S(1)}, f32[1,1,128,128]{3,2,1,0:T(8,128)}, u32[]{:S(2)}, u32[]{:S(2)}) collective-permute-start(f32[1,1,128,128]{3,2,1,0:T(8,128)S(1)} %slice_bitcast_fusion), channel_id=1, source_target_pairs={{0,8},{8,16},{16,24},{24,0},{1,9},{9,17},{17,25},{25,1},{2,10},{10... | collective-permute-start | bytes 196616 | tf_op jit(solution)/shard_map/ppermute | solution.py:94
  11.4 9.4 %collective-permute-start.7 = (f32[1,1,128,128]{3,2,1,0:T(8,128)S(1)}, f32[1,1,128,128]{3,2,1,0:T(8,128)S(1)}, u32[]{:S(2)}, u32[]{:S(2)}) collective-permute-start(f32[1,1,128,128]{3,2,1,0:T(8,128)S(1)} %slice_bitcast_fusion), channel_id=1, source_target_pairs={{0,24},{8,0},{16,8},{24,16},{1,25},{9,1},{17,9},{25,17},{2,26},{10... | collective-permute-start | bytes 196616 | tf_op jit(solution)/shard_map/ppermute | solution.py:99
  13.4 0.9 %copy-start.2 = (bf16[2,256,128]{2,1,0:T(8,128)(2,1)S(1)}, bf16[2,256,128]{2,1,0:T(8,128)(2,1)}, u32[]{:S(2)}) copy-start(bf16[2,256,128]{2,1,0:T(8,128)(2,1)} %param.22) | copy-start | bytes 393220
  16.5 5.2 %collective-permute-start.2 = (f32[1,1,128,128]{3,2,1,0:T(8,128)S(1)}, f32[1,1,128,128]{3,2,1,0:T(8,128)S(1)}, u32[]{:S(2)}, u32[]{:S(2)}) collective-permute-start(f32[1,1,128,128]{3,2,1,0:T(8,128)S(1)} %collective-permute-done), channel_id=1, source_target_pairs={{0,8},{8,16},{16,24},{24,0},{1,9},{9,17},{17,25},{25,1},{2,10},{10... | collective-permute-start | bytes 196616 | tf_op jit(solution)/shard_map/ppermute | solution.py:94
  17.0 7.9 %collective-permute-start.8 = (f32[1,1,128,128]{3,2,1,0:T(8,128)}, f32[1,1,128,128]{3,2,1,0:T(8,128)S(1)}, u32[]{:S(2)}, u32[]{:S(2)}) collective-permute-start(f32[1,1,128,128]{3,2,1,0:T(8,128)} %collective-permute-done.6), channel_id=1, source_target_pairs={{0,8},{8,16},{16,24},{24,0},{1,9},{9,17},{17,25},{25,1},{2,10},{10... | collective-permute-start | bytes 196616 | tf_op jit(solution)/shard_map/ppermute | solution.py:94
  22.0 7.9 %collective-permute-start.3 = (f32[1,1,128,128]{3,2,1,0:T(8,128)S(1)}, f32[1,1,128,128]{3,2,1,0:T(8,128)S(1)}, u32[]{:S(2)}, u32[]{:S(2)}) collective-permute-start(f32[1,1,128,128]{3,2,1,0:T(8,128)S(1)} %get-tuple-element.15), channel_id=1, source_target_pairs={{0,8},{8,16},{16,24},{24,0},{1,9},{9,17},{17,25},{25,1},{2,10},{10... | collective-permute-start | bytes 196616 | tf_op jit(solution)/shard_map/ppermute | solution.py:94
  22.1 11.2 %collective-permute-start.4 = (f32[1,1,128,128]{3,2,1,0:T(8,128)S(1)}, f32[1,1,128,128]{3,2,1,0:T(8,128)S(1)}, u32[]{:S(2)}, u32[]{:S(2)}) collective-permute-start(f32[1,1,128,128]{3,2,1,0:T(8,128)S(1)} %get-tuple-element.15), channel_id=1, source_target_pairs={{0,24},{8,0},{16,8},{24,16},{1,25},{9,1},{17,9},{25,17},{2,26},{10... | collective-permute-start | bytes 196616 | tf_op jit(solution)/shard_map/ppermute | solution.py:99
  24.9 0.8 copy-start.5
  25.8 0.9 %copy-start.3 = (bf16[2,128,256]{2,1,0:T(8,128)(2,1)S(1)}, bf16[2,128,256]{2,1,0:T(8,128)(2,1)}, u32[]{:S(2)}) copy-start(bf16[2,128,256]{2,1,0:T(8,128)(2,1)} %param.23) | copy-start | bytes 393220
  26.9 5.5 %collective-permute-start.9 = (f32[1,1,128,128]{3,2,1,0:T(8,128)S(1)}, f32[1,1,128,128]{3,2,1,0:T(8,128)S(1)}, u32[]{:S(2)}, u32[]{:S(2)}) collective-permute-start(f32[1,1,128,128]{3,2,1,0:T(8,128)S(1)} %get-tuple-element.13), channel_id=1, source_target_pairs={{0,8},{8,16},{16,24},{24,0},{1,9},{9,17},{17,25},{25,1},{2,10},{10... | collective-permute-start | bytes 196616 | tf_op jit(solution)/shard_map/ppermute | solution.py:94
  27.4 6.6 %collective-permute-start.10 = (f32[1,1,128,128]{3,2,1,0:T(8,128)S(1)}, f32[1,1,128,128]{3,2,1,0:T(8,128)S(1)}, u32[]{:S(2)}, u32[]{:S(2)}) collective-permute-start(f32[1,1,128,128]{3,2,1,0:T(8,128)S(1)} %get-tuple-element.13), channel_id=1, source_target_pairs={{0,24},{8,0},{16,8},{24,16},{1,25},{9,1},{17,9},{25,17},{2,26},{10... | collective-permute-start | bytes 196616 | tf_op jit(solution)/shard_map/ppermute | solution.py:99
  29.9 5.2 %collective-permute-start.5 = (f32[1,1,128,128]{3,2,1,0:T(8,128)S(1)}, f32[1,1,128,128]{3,2,1,0:T(8,128)S(1)}, u32[]{:S(2)}, u32[]{:S(2)}) collective-permute-start(f32[1,1,128,128]{3,2,1,0:T(8,128)S(1)} %collective-permute-done.3), channel_id=1, source_target_pairs={{0,8},{8,16},{16,24},{24,0},{1,9},{9,17},{17,25},{25,1},{2,10},{10... | collective-permute-start | bytes 196616 | tf_op jit(solution)/shard_map/ppermute | solution.py:94
  32.4 5.2 %collective-permute-start.11 = (f32[1,1,128,128]{3,2,1,0:T(8,128)S(1)}, f32[1,1,128,128]{3,2,1,0:T(8,128)S(1)}, u32[]{:S(2)}, u32[]{:S(2)}) collective-permute-start(f32[1,1,128,128]{3,2,1,0:T(8,128)S(1)} %collective-permute-done.9), channel_id=1, source_target_pairs={{0,8},{8,16},{16,24},{24,0},{1,9},{9,17},{17,25},{25,1},{2,10},{10... | collective-permute-start | bytes 196616 | tf_op jit(solution)/shard_map/ppermute | solution.py:94
